TPU v7x, 32 devices: a whole 2x2x4 slice. The times are simulated.
32 devices in a mesh: group: 16 (over z, x, core), loop: 2 (over y).
Axes of the slice: x: 2, y: 2, z: 4, core: 2. Of those that a mesh axis runs over, the one named last changes fastest.
Arguments:
- user_factors: bfloat16 [32768, 256], P('group'), may hold values from -1.5 to 1.5
- item_factors: bfloat16 [2048, 256], P('loop'), may hold values from -1.5 to 1.5
- tag_factors: bfloat16 [2048, 256], P('group'), may hold values from -1.5 to 1.5
- ratings: bfloat16 [32768, 2048], P('group', 'loop'), may hold values from -6 to 6
- rating_tiles: int32 [256, 16], P('group', 'loop'), may hold values 0 or 1
- tag_links: bfloat16 [2048, 2048], P('loop', 'group'), may hold values from -6 to 6
- link_tiles: int32 [16, 16], P('loop', 'group'), may hold values 0 or 1
Outputs:
- new_users: bfloat16 [32768, 256], P('group')
- new_items: bfloat16 [2048, 256], P('loop')
- new_tags: bfloat16 [2048, 256], P('group')
Inputs may be any that keep to these rules, and one draw needn't show every extreme that they name: `rating_tiles`: 1 marks a tile of observed entries, 0 an empty tile. `link_tiles`: 1 marks a tile of observed entries, 0 an empty tile.
All inputs are finite; a program needn't handle non-finite values. No bound on the sum of `rating_tiles` or of `link_tiles` on one device may be relied on, other than what follows from the above.
Results may differ from a plain program's by a relative error of at most 0.0034.
Values may be sent and summed in bfloat16 or wider, within the bound.
No kernel may reach another device: no remote copies, remote signals or barrier semaphores. Data moves between devices by JAX's collectives and lax.ppermute only.
A program may use at most 64 MiB of HBM per device.

v0:
```python
import jax
import jax.numpy as jnp
from jax import lax
from jax.sharding import PartitionSpec as P

step_users = 0.015
step_items = 0.004
step_tags = 0.015


def tile_masked(values, tile_flags):
    height, breadth = values.shape
    blocks = values.reshape(height // 128, 128, breadth // 128, 128)
    masked = blocks * tile_flags.astype(jnp.float32)[:, None, :, None]
    return masked.reshape(height, breadth)


def residual_of(observed, row_factors, column_factors, tile_flags):
    predicted = lax.dot_general(
        row_factors, column_factors, (((1,), (1,)), ((), ())), preferred_element_type=jnp.float32
    )
    return tile_masked(observed.astype(jnp.float32) - predicted, tile_flags).astype(jnp.bfloat16)


def transposed_product(first_operand, second_operand):
    return lax.dot_general(
        first_operand, second_operand, (((0,), (0,)), ((), ())), preferred_element_type=jnp.float32
    )


def advance(factors, gradient, rate):
    return (factors.astype(jnp.float32) + rate * gradient).astype(jnp.bfloat16)


def own_share(factors, axis_count, position):
    share_rows = factors.shape[0] // axis_count
    return lax.dynamic_slice_in_dim(factors, position * share_rows, share_rows, 0)


def shards(user_factors, item_factors, tag_factors, ratings, rating_tiles, tag_links, link_tiles):
    link_errors = residual_of(tag_links, item_factors, tag_factors, link_tiles)
    rating_errors = residual_of(ratings, user_factors, item_factors, rating_tiles)
    item_part = transposed_product(rating_errors, user_factors) + jnp.dot(
        link_errors, tag_factors, preferred_element_type=jnp.float32
    )
    user_part = jnp.dot(rating_errors, item_factors, preferred_element_type=jnp.float32)
    tag_part = transposed_product(link_errors, item_factors)
    item_share = lax.psum_scatter(item_part, "group", scatter_dimension=0, tiled=True)
    group_count = lax.axis_size("group")
    group_position = lax.axis_index("group")
    fresh_share = advance(
        own_share(item_factors, group_count, group_position), item_share, step_items
    )
    new_items = lax.all_gather(fresh_share, "group", axis=0, tiled=True)
    user_grad, tag_grad = lax.psum((user_part, tag_part), "loop")
    new_users = advance(user_factors, user_grad, step_users)
    new_tags = advance(tag_factors, tag_grad, step_tags)
    return (new_users, new_items, new_tags)


def solution(mesh):
    in_specs = (
        P("group", None),
        P("loop", None),
        P("group", None),
        P("group", "loop"),
        P("group", "loop"),
        P("loop", "group"),
        P("loop", "group"),
    )
    out_specs = (P("group", None), P("loop", None), P("group", None))
    return jax.shard_map(shards, mesh=mesh, in_specs=in_specs, out_specs=out_specs, check_vma=False)
```

profile of v0, /device:TPU:0, one launch (start us, length us, event | category | flops | bytes accessed | tf_op | source)
XLA Modules:
  0.0 111.5 jit_solution(9205640242450746977)
XLA Ops:
  8.0 0.0 reduce-scatter.2.cloned.1.call-start
  8.0 0.7 convert_element_type.38
  8.7 0.1 copy.10
  8.8 0.7 convert_bitcast_fusion
  9.5 0.1 broadcast_bitcast_fusion
  9.5 0.0 copy-start
  9.5 0.0 copy-start.1
  9.5 0.0 copy-start.2
  9.5 0.6 mul.49
  10.2 0.4 copy-done
  10.6 0.3 copy-done.1
  10.9 1.3 %copy-done.2 = bf16[2048,1024]{1,0:T(8,128)(2,1)S(1)} copy-done((bf16[2048,1024]{1,0:T(8,128)(2,1)S(1)}, bf16[2048,1024]{1,0:T(8,128)(2,1)}, u32[]{:S(2)}) %copy-start.2) | copy-done | bytes 4194328
  12.2 2.0 %fusion = bf16[2048,1024]{1,0:T(8,128)(2,1)S(1)} fusion(f32[256,8,8,128]{3,2,1,0:T(8,128)S(1)} %bitcast.22, bf16[2048,1024]{1,0:T(8,128)(2,1)S(1)} %copy-done.2, bf16[2048,256]{1,0:T(8,128)(2,1)S(1)} %copy-done.1, bf16[1024,256]{1,0:T(8,128)(2,1)S(1)} %copy-done), kind=kOutput, calls=%fused_computation.1 | convolution fusion | flops 1082130432 | bytes 18350080 | tf_op jit(solution)/shard_map/dot_general | solution.py:19
  14.3 0.0 copy-start.3
  14.3 0.0 copy-start.4
  14.3 0.0 copy-start.5
  14.3 1.3 %fusion.4 = f32[1024,256]{1,0:T(8,128)S(1)} fusion(bf16[2048,1024]{1,0:T(8,128)(2,1)S(1)} %fusion, bf16[2048,256]{1,0:T(8,128)(2,1)S(1)} %copy-done.1), kind=kOutput, calls=%fused_computation.12 | convolution fusion | flops 1073741824 | bytes 6291456 | tf_op jit(solution)/shard_map/dot_general | solution.py:26
  15.6 0.6 copy-done.3
  16.2 0.0 copy-done.4
  16.2 0.0 copy-done.5
  16.2 0.3 fusion.2
  16.5 1.2 %convolution_add_fusion = f32[1024,256]{1,0:T(8,128)} fusion(f32[1024,256]{1,0:T(8,128)S(1)} %fusion.4, bf16[1024,128]{1,0:T(8,128)(2,1)S(1)} %fusion.2, bf16[128,256]{1,0:T(8,128)(2,1)S(1)} %copy-done.4), kind=kOutput, calls=%fused_computation.3 | convolution fusion | flops 67371008 | bytes 2424832 | tf_op jit(solution)/shard_map/dot_general | solution.py:43
  17.8 0.0 reduce-scatter.2.cloned.1.call-update
  17.8 0.0 all-reduce.3.cloned.1.call-start
  17.9 0.9 fusion.5
  18.8 4.8 %fusion.3 = f32[2048,256]{1,0:T(8,128)} fusion(bf16[2048,1024]{1,0:T(8,128)(2,1)} %copy-done.3, bf16[1024,256]{1,0:T(8,128)(2,1)S(1)} %copy-done), kind=kOutput, calls=%fused_computation.11 | convolution fusion | flops 1073741824 | bytes 6815744 | tf_op jit(solution)/shard_map/dot_general | solution.py:46
  23.5 0.0 all-reduce.3.cloned.1.call-update
  23.6 54.4 %reduce-scatter.2.cloned.1.call-done = f32[64,256]{1,0:T(8,128)} async-done(((f32[1024,256]{1,0:T(8,128)}), f32[64,256]{1,0:T(8,128)}) %reduce-scatter.2.cloned.1.call-update) | async-done | bytes 65552 | tf_op jit(solution)/shard_map/reduce_scatter | solution.py:48
  78.0 0.9 add_convert_fusion.2
  78.8 20.9 %all_gather.3 = bf16[1024,256]{1,0:T(8,128)(2,1)S(1)} all-gather(bf16[64,256]{1,0:T(8,128)(2,1)S(1)} %add_convert_fusion.2), channel_id=1, replica_groups=mesh['group'=16,'loop'=2] {'group'}, dimensions={0}, use_global_device_ids=true | all-gather | bytes 557056 | tf_op jit(solution)/shard_map/all_gather | solution.py:54
  99.7 0.0 all-reduce.3.cloned.1.call-done
  99.7 0.0 copy-start.6
  99.7 2.9 %add_convert_fusion = bf16[2048,256]{1,0:T(8,128)(2,1)} fusion(f32[2048,256]{1,0:T(8,128)} %get-tuple-element.3, bf16[2048,256]{1,0:T(8,128)(2,1)S(1)} %copy-done.1), kind=kLoop, calls=%fused_computation.2 | loop fusion | flops 2097152 | bytes 4194304 | tf_op jit(solution)/shard_map/convert_element_type | solution.py:32
  102.6 0.0 copy-done.6
  102.6 0.7 add_convert_fusion.1
  103.3 0.8 copy.16
Async XLA Ops:
  8.0 70.0 %reduce-scatter.2.cloned.1.call-start = ((), (), s32[]{:S(2)}) async-start(), calls=%async_computation.1 | async-start | bytes 1114112 | tf_op jit(solution)/shard_map/reduce_scatter | solution.py:48
  9.5 1.0 copy-start
  9.5 1.4 %copy-start.1 = (bf16[2048,256]{1,0:T(8,128)(2,1)S(1)}, bf16[2048,256]{1,0:T(8,128)(2,1)}, u32[]{:S(2)}) copy-start(bf16[2048,256]{1,0:T(8,128)(2,1)} %param.7) | copy-start | bytes 3145732
  9.5 2.7 %copy-start.2 = (bf16[2048,1024]{1,0:T(8,128)(2,1)S(1)}, bf16[2048,1024]{1,0:T(8,128)(2,1)}, u32[]{:S(2)}) copy-start(bf16[2048,1024]{1,0:T(8,128)(2,1)} %param.10) | copy-start | bytes 12582916
  14.3 1.9 %copy-start.3 = (bf16[2048,1024]{1,0:T(8,128)(2,1)}, bf16[2048,1024]{1,0:T(8,128)(2,1)S(1)}, u32[]{:S(2)}) copy-start(bf16[2048,1024]{1,0:T(8,128)(2,1)S(1)} %fusion) | copy-start | bytes 12582916
  14.3 1.9 %copy-start.4 = (bf16[128,256]{1,0:T(8,128)(2,1)S(1)}, bf16[128,256]{1,0:T(8,128)(2,1)}, u32[]{:S(2)}) copy-start(bf16[128,256]{1,0:T(8,128)(2,1)} %param.9) | copy-start | bytes 196612
  14.3 1.9 %copy-start.5 = (bf16[1024,128]{1,0:T(8,128)(2,1)S(1)}, bf16[1024,128]{1,0:T(8,128)(2,1)}, u32[]{:S(2)}) copy-start(bf16[1024,128]{1,0:T(8,128)(2,1)} %param.12) | copy-start | bytes 786436
  17.8 81.9 %all-reduce.3.cloned.1.call-start = ((), (), s32[]{:S(2)}) async-start(), calls=%async_computation.2 | async-start | bytes 4456448 | tf_op jit(solution)/shard_map/psum | solution.py:55
  99.7 2.9 %copy-start.6 = (f32[128,256]{1,0:T(8,128)S(1)}, f32[128,256]{1,0:T(8,128)}, u32[]{:S(2)}) copy-start(f32[128,256]{1,0:T(8,128)} %get-tuple-element.4) | copy-start | bytes 393220
Sparse Core Ops, SparseCore 0:
  17.9 60.0 reduce-scatter.1
Sparse Core Ops, SparseCore 1:
  23.6 68.5 all-reduce.2
where the time goes:
time: 112 us
  waiting for transfers between devices  54.4 us (49%)
  blocking collectives  20.9 us (19%)
  between operations  15.5 us (14%)
  matrix products  10.6 us (9%)
  other arithmetic  5.74 us (5%)
  local copies, waits for them, and re-layouts  4.24 us (4%)
    reduce_scatter x1, waiting for transfers between devices, shards(): lax.psum_scatter(item_part, 'group', scatter_dimension=0, tiled=True)  54.4 us
    all_gather x1, blocking collectives, shards(): new_items = lax.all_gather(fresh_share, 'group', axis=0, tiled=True)  20.9 us
    dot_general x1, matrix products, shards(): jnp.dot(rating_errors, item_factors, preferred_element_type=jnp.float32)  4.76 us
    convert_element_type x3, other arithmetic, advance(): return (factors.astype(jnp.float32) + rate * gradient).astype(jnp.bfloat16)  4.4 us
    unnamed x15, local copies, waits for them, and re-layouts  3.49 us
    dot_general x2, matrix products, residual_of(): lax.dot_general(row_factors, column_factors, (((1,), (1,)), ((), ())), pr...  2.34 us
  transfers between devices with their start and end apart: 2, of which 1 were waited for; matrix products, arithmetic and copies ran while one was open for 6% of the time, Pallas kernels for 0%

commit v1 on v0

--- a/solution.py
+++ b/solution.py
@@ -51,7 +51,15 @@
     fresh_share = advance(
         own_share(item_factors, group_count, group_position), item_share, step_items
     )
-    new_items = lax.all_gather(fresh_share, "group", axis=0, tiled=True)
+    ways, here, lap = (lax.axis_size("group"), lax.axis_index("group"), fresh_share.shape[0])
+    line, have = (fresh_share, 1)
+    while have < ways:
+        line = jnp.concatenate(
+            [line, lax.ppermute(line, "group", [(d, (d - have) % ways) for d in range(ways)])],
+            axis=0,
+        )
+        have = 2 * have
+    new_items = jnp.roll(line, here * lap, axis=0)
     user_grad, tag_grad = lax.psum((user_part, tag_part), "loop")
     new_users = advance(user_factors, user_grad, step_users)
     new_tags = advance(tag_factors, tag_grad, step_tags)

time: 112 us -> 119 us (1.062)
  blocking collectives: 20.9 us -> 0 us
  waiting for transfers between devices: 54.4 us -> 75 us
  starting transfers between devices: 0.08 us -> 7 us
    all_gather x1 -> x0, blocking collectives: 20.9 us -> none  [shards(): new_items = lax.all_gather(fresh_share, 'group', axis=0, tiled=True)]
    ppermute x0 -> x4, waiting for transfers between devices: none -> 20.5 us  [shards(): lax.ppermute(line, 'group', [(d, (d - have) % ways) for d in range(ways)])]
    ppermute x0 -> x4, starting transfers between devices: none -> 6.92 us  [shards(): lax.ppermute(line, 'group', [(d, (d - have) % ways) for d in range(ways)])]
    convert_element_type x3 -> x2, other arithmetic: 4.4 us -> 3.55 us  [advance(): return (factors.astype(jnp.float32) + rate * gradient).astype(jnp.bfloat16)]
    unnamed x15 -> x22, local copies, waits for them, and re-layouts: 3.49 us -> 2.77 us
  transfers between devices with their start and end apart: 2 -> 6, of which waited for: 1 -> 5; matrix products, arithmetic and copies ran while one was open for 6% -> 6% of each run, Pallas kernels for 0% -> 0%
where the time goes in v1:
time: 119 us; the launch traced here: 118 us
  waiting for transfers between devices  75 us (63%)
  between operations  15.6 us (13%)
  matrix products  10.6 us (9%)
  starting transfers between devices  7 us (6%)
  other arithmetic  5.78 us (5%)
  local copies, waits for them, and re-layouts  4.37 us (4%)
    reduce_scatter x1, waiting for transfers between devices, shards(): lax.psum_scatter(item_part, 'group', scatter_dimension=0, tiled=True)  54.4 us
    ppermute x4, waiting for transfers between devices, shards(): lax.ppermute(line, 'group', [(d, (d - have) % ways) for d in range(ways)])  20.5 us
    ppermute x4, starting transfers between devices, shards(): lax.ppermute(line, 'group', [(d, (d - have) % ways) for d in range(ways)])  6.92 us
    dot_general x1, matrix products, shards(): jnp.dot(rating_errors, item_factors, preferred_element_type=jnp.float32)  4.78 us
    convert_element_type x2, other arithmetic, advance(): return (factors.astype(jnp.float32) + rate * gradient).astype(jnp.bfloat16)  3.55 us
    unnamed x22, local copies, waits for them, and re-layouts  2.77 us
  transfers between devices with their start and end apart: 6, of which 5 were waited for; matrix products, arithmetic and copies ran while one was open for 6% of the time, Pallas kernels for 0%

profile of v1, /device:TPU:0, one launch (start us, length us, event | category | flops | bytes accessed | tf_op | source)
XLA Modules:
  0.0 118.3 jit_solution(6647611687941753158)
XLA Ops:
  8.0 0.0 reduce-scatter.2.cloned.1.call-start
  8.0 0.7 convert_element_type.38
  8.7 0.1 copy.10
  8.8 0.7 convert_bitcast_fusion
  9.5 0.1 broadcast_bitcast_fusion
  9.5 0.0 copy-start
  9.5 0.0 copy-start.1
  9.5 0.0 copy-start.2
  9.5 0.6 mul.50
  10.2 0.4 copy-done
  10.6 0.3 copy-done.1
  10.9 1.3 %copy-done.2 = bf16[2048,1024]{1,0:T(8,128)(2,1)S(1)} copy-done((bf16[2048,1024]{1,0:T(8,128)(2,1)S(1)}, bf16[2048,1024]{1,0:T(8,128)(2,1)}, u32[]{:S(2)}) %copy-start.2) | copy-done | bytes 4194328
  12.2 2.0 %fusion = bf16[2048,1024]{1,0:T(8,128)(2,1)S(1)} fusion(f32[256,8,8,128]{3,2,1,0:T(8,128)S(1)} %bitcast.22, bf16[2048,1024]{1,0:T(8,128)(2,1)S(1)} %copy-done.2, bf16[2048,256]{1,0:T(8,128)(2,1)S(1)} %copy-done.1, bf16[1024,256]{1,0:T(8,128)(2,1)S(1)} %copy-done), kind=kOutput, calls=%fused_computation.1 | convolution fusion | flops 1082130432 | bytes 18350080 | tf_op jit(solution)/shard_map/dot_general | solution.py:19
  14.3 0.0 copy-start.3
  14.3 0.0 copy-start.4
  14.3 0.0 copy-start.5
  14.3 1.3 %fusion.4 = f32[1024,256]{1,0:T(8,128)S(1)} fusion(bf16[2048,1024]{1,0:T(8,128)(2,1)S(1)} %fusion, bf16[2048,256]{1,0:T(8,128)(2,1)S(1)} %copy-done.1), kind=kOutput, calls=%fused_computation.26 | convolution fusion | flops 1073741824 | bytes 6291456 | tf_op jit(solution)/shard_map/dot_general | solution.py:26
  15.6 0.6 copy-done.3
  16.2 0.0 copy-done.4
  16.2 0.0 copy-done.5
  16.2 0.3 fusion.2
  16.5 1.2 %convolution_add_fusion = f32[1024,256]{1,0:T(8,128)} fusion(f32[1024,256]{1,0:T(8,128)S(1)} %fusion.4, bf16[1024,128]{1,0:T(8,128)(2,1)S(1)} %fusion.2, bf16[128,256]{1,0:T(8,128)(2,1)S(1)} %copy-done.4), kind=kOutput, calls=%fused_computation.3 | convolution fusion | flops 67371008 | bytes 2424832 | tf_op jit(solution)/shard_map/dot_general | solution.py:43
  17.8 0.0 reduce-scatter.2.cloned.1.call-update
  17.8 0.0 all-reduce.3.cloned.1.call-start
  17.9 0.9 fusion.5
  18.8 4.8 %fusion.3 = f32[2048,256]{1,0:T(8,128)} fusion(bf16[2048,1024]{1,0:T(8,128)(2,1)} %copy-done.3, bf16[1024,256]{1,0:T(8,128)(2,1)S(1)} %copy-done), kind=kOutput, calls=%fused_computation.25 | convolution fusion | flops 1073741824 | bytes 6815744 | tf_op jit(solution)/shard_map/dot_general | solution.py:46
  23.5 0.0 all-reduce.3.cloned.1.call-update
  23.6 54.4 %reduce-scatter.2.cloned.1.call-done = f32[64,256]{1,0:T(8,128)} async-done(((f32[1024,256]{1,0:T(8,128)}), f32[64,256]{1,0:T(8,128)}) %reduce-scatter.2.cloned.1.call-update) | async-done | bytes 65552 | tf_op jit(solution)/shard_map/reduce_scatter | solution.py:48
  78.0 0.9 constant_dynamic-update-slice_fusion.9
  78.8 0.2 collective-permute-start
  79.0 1.6 %collective-permute-done = bf16[64,256]{1,0:T(8,128)(2,1)S(1)} collective-permute-done((bf16[64,256]{1,0:T(8,128)(2,1)S(1)}, bf16[64,256]{1,0:T(8,128)(2,1)S(1)}, u32[]{:S(2)}, u32[]{:S(2)}) %collective-permute-start) | collective-permute-done | bytes 32800 | tf_op jit(solution)/shard_map/ppermute | solution.py:58
  80.6 2.2 %collective-permute-start.1 = (bf16[128,256]{1,0:T(8,128)(2,1)S(1)}, bf16[128,256]{1,0:T(8,128)(2,1)S(1)}, u32[]{:S(2)}, u32[]{:S(2)}) collective-permute-start(bf16[128,256]{1,0:T(8,128)(2,1)S(1)} %pad_maximum_fusion.2), channel_id=1, source_target_pairs={{0,28},{2,30},{4,0},{6,2},{8,4},{10,6},{12,8},{14,10},{16,12},{18,... | collective-permute-start | bytes 196616 | tf_op jit(solution)/shard_map/ppermute | solution.py:58
  82.9 2.0 %collective-permute-done.1 = bf16[128,256]{1,0:T(8,128)(2,1)S(1)} collective-permute-done((bf16[128,256]{1,0:T(8,128)(2,1)S(1)}, bf16[128,256]{1,0:T(8,128)(2,1)S(1)}, u32[]{:S(2)}, u32[]{:S(2)}) %collective-permute-start.1) | collective-permute-done | bytes 65568 | tf_op jit(solution)/shard_map/ppermute | solution.py:58
  84.9 2.5 %collective-permute-start.2 = (bf16[256,256]{1,0:T(8,128)(2,1)S(1)}, bf16[256,256]{1,0:T(8,128)(2,1)S(1)}, u32[]{:S(2)}, u32[]{:S(2)}) collective-permute-start(bf16[256,256]{1,0:T(8,128)(2,1)S(1)} %pad_maximum_fusion.1), channel_id=1, source_target_pairs={{0,24},{2,26},{4,28},{6,30},{8,0},{10,2},{12,4},{14,6},{16,8},{18,... | collective-permute-start | bytes 393224 | tf_op jit(solution)/shard_map/ppermute | solution.py:58
  87.4 3.6 %collective-permute-done.2 = bf16[256,256]{1,0:T(8,128)(2,1)S(1)} collective-permute-done((bf16[256,256]{1,0:T(8,128)(2,1)S(1)}, bf16[256,256]{1,0:T(8,128)(2,1)S(1)}, u32[]{:S(2)}, u32[]{:S(2)}) %collective-permute-start.2) | collective-permute-done | bytes 131104 | tf_op jit(solution)/shard_map/ppermute | solution.py:58
  91.0 2.0 %collective-permute-start.3 = (bf16[512,256]{1,0:T(8,128)(2,1)S(1)}, bf16[512,256]{1,0:T(8,128)(2,1)S(1)}, u32[]{:S(2)}, u32[]{:S(2)}) collective-permute-start(bf16[512,256]{1,0:T(8,128)(2,1)S(1)} %pad_maximum_fusion), channel_id=1, source_target_pairs={{0,16},{2,18},{4,20},{6,22},{8,24},{10,26},{12,28},{14,30},{16,0},... | collective-permute-start | bytes 786440 | tf_op jit(solution)/shard_map/ppermute | solution.py:58
  93.0 13.3 %collective-permute-done.3 = bf16[512,256]{1,0:T(8,128)(2,1)S(1)} collective-permute-done((bf16[512,256]{1,0:T(8,128)(2,1)S(1)}, bf16[512,256]{1,0:T(8,128)(2,1)S(1)}, u32[]{:S(2)}, u32[]{:S(2)}) %collective-permute-start.3) | collective-permute-done | bytes 262176 | tf_op jit(solution)/shard_map/ppermute | solution.py:58
  106.5 0.8 constant_dynamic-slice_fusion
  107.3 0.0 all-reduce.3.cloned.1.call-done
  107.3 0.0 copy-start.6
  107.3 2.9 %add_convert_fusion = bf16[2048,256]{1,0:T(8,128)(2,1)} fusion(f32[2048,256]{1,0:T(8,128)} %get-tuple-element.3, bf16[2048,256]{1,0:T(8,128)(2,1)S(1)} %copy-done.1), kind=kLoop, calls=%fused_computation.2 | loop fusion | flops 2097152 | bytes 4194304 | tf_op jit(solution)/shard_map/convert_element_type | solution.py:32
  110.2 0.0 copy-done.6
  110.2 0.7 add_convert_fusion.1
  (12 shorter events, 0.1 us)
Async XLA Ops:
  8.0 70.0 %reduce-scatter.2.cloned.1.call-start = ((), (), s32[]{:S(2)}) async-start(), calls=%async_computation.1 | async-start | bytes 1114112 | tf_op jit(solution)/shard_map/reduce_scatter | solution.py:48
  9.5 1.0 copy-start
  9.5 1.4 %copy-start.1 = (bf16[2048,256]{1,0:T(8,128)(2,1)S(1)}, bf16[2048,256]{1,0:T(8,128)(2,1)}, u32[]{:S(2)}) copy-start(bf16[2048,256]{1,0:T(8,128)(2,1)} %param.7) | copy-start | bytes 3145732
  9.5 2.7 %copy-start.2 = (bf16[2048,1024]{1,0:T(8,128)(2,1)S(1)}, bf16[2048,1024]{1,0:T(8,128)(2,1)}, u32[]{:S(2)}) copy-start(bf16[2048,1024]{1,0:T(8,128)(2,1)} %param.10) | copy-start | bytes 12582916
  14.3 1.9 %copy-start.3 = (bf16[2048,1024]{1,0:T(8,128)(2,1)}, bf16[2048,1024]{1,0:T(8,128)(2,1)S(1)}, u32[]{:S(2)}) copy-start(bf16[2048,1024]{1,0:T(8,128)(2,1)S(1)} %fusion) | copy-start | bytes 12582916
  14.3 1.9 %copy-start.4 = (bf16[128,256]{1,0:T(8,128)(2,1)S(1)}, bf16[128,256]{1,0:T(8,128)(2,1)}, u32[]{:S(2)}) copy-start(bf16[128,256]{1,0:T(8,128)(2,1)} %param.9) | copy-start | bytes 196612
  14.3 1.9 %copy-start.5 = (bf16[1024,128]{1,0:T(8,128)(2,1)S(1)}, bf16[1024,128]{1,0:T(8,128)(2,1)}, u32[]{:S(2)}) copy-start(bf16[1024,128]{1,0:T(8,128)(2,1)} %param.12) | copy-start | bytes 786436
  17.8 89.5 %all-reduce.3.cloned.1.call-start = ((), (), s32[]{:S(2)}) async-start(), calls=%async_computation.2 | async-start | bytes 4456448 | tf_op jit(solution)/shard_map/psum | solution.py:63
  78.8 1.8 %collective-permute-start = (bf16[64,256]{1,0:T(8,128)(2,1)S(1)}, bf16[64,256]{1,0:T(8,128)(2,1)S(1)}, u32[]{:S(2)}, u32[]{:S(2)}) collective-permute-start(bf16[64,256]{1,0:T(8,128)(2,1)S(1)} %get-tuple-element.6), channel_id=1, source_target_pairs={{0,30},{2,0},{4,2},{6,4},{8,6},{10,8},{12,10},{14,12},{16,14},{18,... | collective-permute-start | bytes 98312 | tf_op jit(solution)/shard_map/ppermute | solution.py:58
  80.6 4.3 %collective-permute-start.1 = (bf16[128,256]{1,0:T(8,128)(2,1)S(1)}, bf16[128,256]{1,0:T(8,128)(2,1)S(1)}, u32[]{:S(2)}, u32[]{:S(2)}) collective-permute-start(bf16[128,256]{1,0:T(8,128)(2,1)S(1)} %pad_maximum_fusion.2), channel_id=1, source_target_pairs={{0,28},{2,30},{4,0},{6,2},{8,4},{10,6},{12,8},{14,10},{16,12},{18,... | collective-permute-start | bytes 196616 | tf_op jit(solution)/shard_map/ppermute | solution.py:58
  84.9 6.1 %collective-permute-start.2 = (bf16[256,256]{1,0:T(8,128)(2,1)S(1)}, bf16[256,256]{1,0:T(8,128)(2,1)S(1)}, u32[]{:S(2)}, u32[]{:S(2)}) collective-permute-start(bf16[256,256]{1,0:T(8,128)(2,1)S(1)} %pad_maximum_fusion.1), channel_id=1, source_target_pairs={{0,24},{2,26},{4,28},{6,30},{8,0},{10,2},{12,4},{14,6},{16,8},{18,... | collective-permute-start | bytes 393224 | tf_op jit(solution)/shard_map/ppermute | solution.py:58
  91.0 15.4 %collective-permute-start.3 = (bf16[512,256]{1,0:T(8,128)(2,1)S(1)}, bf16[512,256]{1,0:T(8,128)(2,1)S(1)}, u32[]{:S(2)}, u32[]{:S(2)}) collective-permute-start(bf16[512,256]{1,0:T(8,128)(2,1)S(1)} %pad_maximum_fusion), channel_id=1, source_target_pairs={{0,16},{2,18},{4,20},{6,22},{8,24},{10,26},{12,28},{14,30},{16,0},... | collective-permute-start | bytes 786440 | tf_op jit(solution)/shard_map/ppermute | solution.py:58
  107.3 2.9 %copy-start.6 = (f32[128,256]{1,0:T(8,128)S(1)}, f32[128,256]{1,0:T(8,128)}, u32[]{:S(2)}) copy-start(f32[128,256]{1,0:T(8,128)} %get-tuple-element.4) | copy-start | bytes 393220
Sparse Core Ops, SparseCore 0:
  17.9 60.0 reduce-scatter.1
Sparse Core Ops, SparseCore 1:
  23.7 68.5 all-reduce.2
